TPU v7x, 32 devices: a whole 2x2x4 slice. The times are simulated.
32 devices in a mesh: shot: 4 (over y, core), mesh: 8 (over z, x).
Axes of the slice: x: 2, y: 2, z: 4, core: 2. Of those that a mesh axis runs over, the one named last changes fastest.
Arguments:
- adjoint_state: float32 [4, 13, 35, 1024], P('shot', None, None, 'mesh'), may hold values from -6 to 6
- forward_states: float32 [4, 2, 13, 35, 1024], P('shot', None, None, None, 'mesh'), may hold values from -6 to 6
- material: float32 [6, 35, 1024], P(None, None, 'mesh'), may hold values from 0.5 to 2
- coupling: float32 [3, 6, 13, 13], replicated, may hold values from -0.375 to 0.375
- metric: float32 [3, 3, 1024], P(None, None, 'mesh'), may hold values from -4 to 4
- face_normals: float32 [3, 4, 1024], P(None, None, 'mesh'), may hold values from -4 to 4
- face_scale: float32 [4, 1024], P(None, 'mesh'), may hold values from 1 to 3
- face_neighbours: int32 [4, 1024], P(None, 'mesh'), may hold values from 0 to 639, as said below
- face_orientation: int32 [4, 1024], P(None, 'mesh'), may hold values from 0 to 5
- send_faces: int32 [1024], P('mesh'), may hold values from 0 to 511, as said below
- history_steps: float32 [5, 6, 35, 1024], P(None, None, None, 'mesh')
- history_changes: float32 [5, 6, 35, 1024], P(None, None, None, 'mesh'), as said below
Outputs:
- adjoint_final: float32 [4, 13, 35, 1024], P('shot', None, None, 'mesh')
- direction: float32 [6, 35, 1024], P(None, None, ('mesh', 'shot'))
Inputs may be any that keep to these rules, and one draw needn't show every extreme that they name: `face_neighbours`: local faces of a partition are numbered x * 128 + e. Each face either forms a pair with another local face (each names the other) or reads exactly one of the 128 ghost slots, and every ghost slot is read by exactly one face; on every partition the face that reads slot 512 + j is send_faces[j] and the face that reads slot 576 + j is send_faces[64 + j]. `send_faces`: the 128 entries of one partition are distinct local face numbers. `history_changes`: for every stored pair, s_i . y_i is positive.
All inputs are finite; a program needn't handle non-finite values.
Results may differ from a plain program's by a relative error of at most 0.0003.
Values sent between devices are 32-bit elements; how exact they have to be, the bound alone decides.
No kernel may reach another device: no remote copies, remote signals or barrier semaphores. Data moves between devices by JAX's collectives and lax.ppermute only.
A program may use at most 64 MiB of HBM per device.

v0:
```python
import math
import jax
import jax.numpy as jnp
import numpy as np
from jax import lax
from jax.sharding import PartitionSpec as P

HIGH = lax.Precision.HIGHEST
STEP_SIZE = 0.02


def padded(x, sides, width):
    for axis, dim in sides:
        devices, length = (lax.axis_size(axis), x.shape[dim])
        up = [(i, (i + 1) % devices) for i in range(devices - 1)]
        down = [(j, i) for i, j in up]
        last = lax.slice_in_dim(x, length - width, length, axis=dim)
        first = lax.slice_in_dim(x, 0, width, axis=dim)
        before = lax.ppermute(last, axis, up)
        after = lax.ppermute(first, axis, down)
        x = jnp.concatenate([before, x, after], axis=dim)
    return x


def invert_matrix(matrix):
    order_count = matrix.shape[0]
    working = np.concatenate([matrix * 1.0, np.eye(order_count)], axis=1)
    for column in range(order_count):
        pivot_row = column + int(np.argmax(np.abs(working[column:, column])))
        working[[column, pivot_row]] = working[[pivot_row, column]]
        working[column] = working[column] / working[column, column]
        for target in range(order_count):
            if target != column:
                working[target] = working[target] - working[target, column] * working[column]
    return working[:, order_count:]


def basis_tables():
    points = [
        (across, along, upward)
        for upward in range(5)
        for along in range(5 - upward)
        for across in range(5 - upward - along)
    ]
    exponents = np.array(points) * 1.0
    coords = exponents / 4.0
    vander = np.prod(coords[:, None, :] ** exponents[None, :, :], axis=2)
    inverse = invert_matrix(vander)
    derivs = []
    for direction_axis in range(3):
        lowered = np.maximum(exponents - np.eye(3)[direction_axis], 0.0)
        slopes = exponents[None, :, direction_axis] * np.prod(
            coords[:, None, :] ** lowered[None, :, :], axis=2
        )
        derivs.append(slopes @ inverse)
    moments = np.array(
        [
            [
                math.factorial(first[0] + second[0])
                * math.factorial(first[1] + second[1])
                * math.factorial(first[2] + second[2])
                / math.factorial(sum(first) + sum(second) + 3)
                for second in points
            ]
            for first in points
        ]
    )
    mass_matrix = inverse.T @ moments @ inverse
    lattice = [(across, along) for along in range(5) for across in range(5 - along)]
    lattice_powers = np.array(lattice) * 1.0
    face_vander = np.prod((lattice_powers / 4.0)[:, None, :] ** lattice_powers[None, :, :], axis=2)
    face_inverse = invert_matrix(face_vander)
    face_moments = np.array(
        [
            [
                math.factorial(first[0] + second[0])
                * math.factorial(first[1] + second[1])
                / math.factorial(sum(first) + sum(second) + 2)
                for second in lattice
            ]
            for first in lattice
        ]
    )
    face_mass = face_inverse.T @ face_moments @ face_inverse
    numbers = {point: number for number, point in enumerate(points)}
    face_points = [
        [(across, along, 0) for across, along in lattice],
        [(across, 0, along) for across, along in lattice],
        [(0, across, along) for across, along in lattice],
        [(across, along, 4 - across - along) for across, along in lattice],
    ]
    face_nodes = np.array(
        [[numbers[point] for point in listing] for listing in face_points], np.int32
    )
    mass_inverse = invert_matrix(mass_matrix)
    lift_tables = []
    for face_number in range(4):
        selector = np.eye(35)[face_nodes[face_number]]
        lift_tables.append(mass_inverse @ selector.T @ face_mass)
    orderings = [(0, 1, 2), (1, 2, 0), (2, 0, 1), (1, 0, 2), (0, 2, 1), (2, 1, 0)]
    lattice_numbers = {point: number for number, point in enumerate(lattice)}
    triples = [(across, along, 4 - across - along) for across, along in lattice]
    turn_nodes = np.array(
        [
            [lattice_numbers[triple[ordering[0]], triple[ordering[1]]] for triple in triples]
            for ordering in orderings
        ],
        np.int32,
    )
    return (
        jnp.asarray(np.stack(derivs), jnp.float32),
        jnp.asarray(np.stack(lift_tables), jnp.float32),
        face_nodes,
        turn_nodes,
    )


def spatial_of(field, metric, derivs):
    reference_grads = jnp.einsum("rab,fbe->rfae", derivs, field, precision=HIGH)
    rows = []
    for direction_axis in range(3):
        total = metric[0, direction_axis] * reference_grads[0]
        total = total + metric[1, direction_axis] * reference_grads[1]
        total = total + metric[2, direction_axis] * reference_grads[2]
        rows.append(total)
    return jnp.stack(rows)


def volume_term(adjoint, material, coupling, metric, derivs):
    spatial = spatial_of(adjoint, metric, derivs)
    mixing = jnp.einsum("dpfg,dfae->pgae", coupling, spatial, precision=HIGH)
    return jnp.sum(material[:, None] * mixing, axis=0)


def kernel_term(adjoint, forward, coupling, metric, derivs):
    spatial = spatial_of(forward, metric, derivs)
    mixing = jnp.einsum("dpfg,dgae->pfae", coupling, spatial, precision=HIGH)
    return jnp.sum(mixing * adjoint[None], axis=1)


def surface_term(jump_trace, face_material, face_normals, face_scale, coupling, lift_tables):
    weighted = face_normals[:, None, None] * jump_trace[None]
    mixing = jnp.einsum("dpfg,dfnxe->pgnxe", coupling, weighted, precision=HIGH)
    face_flux = 0.5 * jnp.sum(face_material[:, None] * mixing, axis=0) + 0.5 * jump_trace
    return jnp.einsum(
        "xan,fnxe->fae", lift_tables, face_flux * face_scale[None, None], precision=HIGH
    )


def search_direction(total_grad, step_rows, change_rows, combine_sums):
    pairs = step_rows.shape[0]
    summed = combine_sums(
        jnp.concatenate(
            [
                jnp.sum(step_rows * change_rows, axis=(1, 2, 3)),
                jnp.sum(change_rows[pairs - 1] * change_rows[pairs - 1])[None],
            ]
        )
    )
    curvature = summed[:pairs]
    alphas = [None] * pairs
    work = total_grad
    for slot in reversed(range(pairs)):
        alphas[slot] = combine_sums(jnp.sum(step_rows[slot] * work)) / curvature[slot]
        work = work - alphas[slot] * change_rows[slot]
    work = curvature[pairs - 1] / summed[pairs] * work
    for slot in range(pairs):
        beta_now = combine_sums(jnp.sum(change_rows[slot] * work)) / curvature[slot]
        work = work + (alphas[slot] - beta_now) * step_rows[slot]
    return -work


def shards(
    adjoint_state,
    forward_states,
    material,
    coupling,
    metric,
    face_normals,
    face_scale,
    face_neighbours,
    face_orientation,
    send_faces,
    history_steps,
    history_changes,
):
    derivs, lift_tables, face_nodes, turn_nodes = basis_tables()
    fields = adjoint_state.shape[1]
    elements = adjoint_state.shape[3]
    node_count = material.shape[1]
    params = material.shape[0]
    face_width = face_nodes.shape[1]
    border = send_faces.shape[0] // 2
    slot_count = 4 * elements + 2 * border
    adjoint = adjoint_state[0]
    face_material = material[:, face_nodes.T, :]
    neighbours = face_neighbours.reshape(-1)
    orient = face_orientation.reshape(-1)
    node_pick = jnp.zeros((face_width, 4 * elements), jnp.int32)
    for option in range(turn_nodes.shape[0]):
        node_pick = (
            node_pick
            + (orient == option).astype(jnp.int32)[None, :]
            * jnp.asarray(turn_nodes[option], jnp.int32)[:, None]
        )
    flat_index = (node_pick * slot_count + neighbours[None, :]).reshape(-1)
    gradient = jnp.zeros((params, node_count, elements), jnp.float32)
    for step_index in range(forward_states.shape[1]):
        inner_trace = adjoint[:, face_nodes.T, :]
        flat_trace = inner_trace.reshape(fields, face_width, 4 * elements)
        sent_traces = flat_trace[:, :, send_faces]
        extended = padded(sent_traces, (("mesh", 2),), border)
        ghosts = jnp.concatenate(
            [flat_trace, extended[:, :, :border], extended[:, :, 3 * border :]], axis=2
        )
        turned = ghosts.reshape(fields, face_width * slot_count)[:, flat_index]
        jump_trace = turned.reshape(fields, face_width, 4, elements) - inner_trace
        change = volume_term(adjoint, material, coupling, metric, derivs) + surface_term(
            jump_trace, face_material, face_normals, face_scale, coupling, lift_tables
        )
        adjoint = adjoint + STEP_SIZE * change
        gradient = gradient + STEP_SIZE * kernel_term(
            adjoint, forward_states[0, step_index], coupling, metric, derivs
        )
    total_grad = lax.psum(gradient, "shot")

    def combine_sums(values):
        return lax.psum(values, "mesh")

    result = search_direction(total_grad, history_steps, history_changes, combine_sums)
    share_width = elements // lax.axis_size("shot")
    result = lax.dynamic_slice_in_dim(result, lax.axis_index("shot") * share_width, share_width, 2)
    return (adjoint[None], result)


def solution(mesh):
    placed = (
        P("shot", None, None, "mesh"),
        P("shot", None, None, None, "mesh"),
        P(None, None, "mesh"),
        P(),
        P(None, None, "mesh"),
        P(None, None, "mesh"),
        P(None, "mesh"),
        P(None, "mesh"),
        P(None, "mesh"),
        P("mesh"),
        P(None, None, None, "mesh"),
        P(None, None, None, "mesh"),
    )
    return jax.shard_map(
        shards,
        mesh=mesh,
        in_specs=placed,
        out_specs=(P("shot", None, None, "mesh"), P(None, None, ("mesh", "shot"))),
        check_vma=False,
    )
```

profile of v0, /device:TPU:0, one launch (start us, length us, event | category | flops | bytes accessed | tf_op | source)
XLA Modules:
  0.0 404.9 jit_solution(5043594300675908869)
XLA Ops:
  9.8 3.6 copy.157
  13.5 3.8 gather_fusion.2
  21.2 6.3 %collective-permute-start = (f32[13,15,64]{1,0,2:T(8,128)}, f32[13,15,64]{1,0,2:T(8,128)}, u32[]{:S(2)}, u32[]{:S(2)}) collective-permute-start(f32[13,15,64]{1,0,2:T(8,128)} %get-tuple-element.22), channel_id=1, source_target_pairs={{0,1},{1,2},{2,3},{3,4},{4,5},{5,6},{6,7},{8,9},{9,10},{10,11},{11... | collective-permute-start | bytes 149768 | tf_op jit(solution)/shard_map/ppermute | solution.py:19
  40.8 7.6 %collective-permute-done = f32[13,15,64]{1,0,2:T(8,128)} collective-permute-done((f32[13,15,64]{1,0,2:T(8,128)}, f32[13,15,64]{1,0,2:T(8,128)}, u32[]{:S(2)}, u32[]{:S(2)}) %collective-permute-start) | collective-permute-done | bytes 49952 | tf_op jit(solution)/shard_map/ppermute | solution.py:19
  53.0 17.3 %gather_fusion.3 = f32[7680,13]{1,0:T(8,128)} fusion(f32[13,9600]{0,1:T(8,128)} %bitcast.349, s32[8192]{0:T(1024)S(1)} %pad_clamp_fusion), kind=kCustom, calls=%fused_computation.3 | custom fusion | bytes 829440 | tf_op jit(solution)/shard_map/gather | solution.py:216
  73.1 3.6 fusion.1
  81.2 3.6 copy.170
  84.8 3.9 gather_fusion.5
  92.2 5.8 %collective-permute-start.2 = (f32[13,15,64]{1,0,2:T(8,128)}, f32[13,15,64]{1,0,2:T(8,128)}, u32[]{:S(2)}, u32[]{:S(2)}) collective-permute-start(f32[13,15,64]{1,0,2:T(8,128)} %get-tuple-element.20), channel_id=1, source_target_pairs={{0,1},{1,2},{2,3},{3,4},{4,5},{5,6},{6,7},{8,9},{9,10},{10,11},{11... | collective-permute-start | bytes 149768 | tf_op jit(solution)/shard_map/ppermute | solution.py:19
  103.0 4.5 %collective-permute-done.3 = f32[13,15,64]{1,0,2:T(8,128)} collective-permute-done((f32[13,15,64]{1,0,2:T(8,128)S(1)}, f32[13,15,64]{1,0,2:T(8,128)}, u32[]{:S(2)}, u32[]{:S(2)}) %collective-permute-start.3) | collective-permute-done | bytes 49952 | tf_op jit(solution)/shard_map/ppermute | solution.py:20
  108.7 10.1 %collective-permute-done.2 = f32[13,15,64]{1,0,2:T(8,128)} collective-permute-done((f32[13,15,64]{1,0,2:T(8,128)}, f32[13,15,64]{1,0,2:T(8,128)}, u32[]{:S(2)}, u32[]{:S(2)}) %collective-permute-start.2) | collective-permute-done | bytes 49952 | tf_op jit(solution)/shard_map/ppermute | solution.py:19
  120.2 3.2 copy.173
  123.5 17.3 %gather_fusion.6 = f32[7680,13]{1,0:T(8,128)} fusion(f32[13,9600]{0,1:T(8,128)} %bitcast.348, s32[8192]{0:T(1024)S(1)} %pad_clamp_fusion), kind=kCustom, calls=%fused_computation.6 | custom fusion | bytes 829440 | tf_op jit(solution)/shard_map/gather | solution.py:216
  150.6 31.2 %all-reduce.3.cloned.1.call-done = f32[6,35,128]{2,0,1:T(8,128)} async-done(((f32[6,35,128]{2,0,1:T(8,128)}), f32[6,35,128]{2,0,1:T(8,128)}) %all-reduce.3.cloned.1.call-update) | async-done | bytes 107536 | tf_op jit(solution)/shard_map/psum | solution.py:225
  183.3 22.0 %all-reduce = (f32[]{:T(128)}, f32[6]{0:T(128)S(1)}) all-reduce(f32[]{:T(128)} %multiply_reduce_fusion.1, f32[6]{0:T(128)S(1)} %pad_maximum_fusion.2), channel_id=1, replica_groups=mesh['shot'=4,'mesh'=8] {'mesh'}, use_global_device_ids=true, to_apply=%region_11.0 | all-reduce | flops 7 | bytes 56 | tf_op jit(solution)/shard_map/psum | solution.py:228
  208.8 17.8 %psum.87 = f32[]{:T(128)} all-reduce(f32[]{:T(128)} %fusion.63), channel_id=1, replica_groups=mesh['shot'=4,'mesh'=8] {'mesh'}, use_global_device_ids=true, to_apply=%region_13.0 | all-reduce | flops 1 | bytes 8 | tf_op jit(solution)/shard_map/psum | solution.py:228
  229.5 19.7 %psum.88 = f32[]{:T(128)} all-reduce(f32[]{:T(128)} %get-tuple-element.18), channel_id=1, replica_groups=mesh['shot'=4,'mesh'=8] {'mesh'}, use_global_device_ids=true, to_apply=%region_15.0 | all-reduce | flops 1 | bytes 8 | tf_op jit(solution)/shard_map/psum | solution.py:228
  251.2 17.8 %psum.89 = f32[]{:T(128)} all-reduce(f32[]{:T(128)} %fusion.47), channel_id=1, replica_groups=mesh['shot'=4,'mesh'=8] {'mesh'}, use_global_device_ids=true, to_apply=%region_17.0 | all-reduce | flops 1 | bytes 8 | tf_op jit(solution)/shard_map/psum | solution.py:228
  271.0 19.7 %psum.90 = f32[]{:T(128)} all-reduce(f32[]{:T(128)} %get-tuple-element.16), channel_id=1, replica_groups=mesh['shot'=4,'mesh'=8] {'mesh'}, use_global_device_ids=true, to_apply=%region_19.0 | all-reduce | flops 1 | bytes 8 | tf_op jit(solution)/shard_map/psum | solution.py:228
  294.1 17.8 %psum.91 = f32[]{:T(128)} all-reduce(f32[]{:T(128)} %fusion.36), channel_id=1, replica_groups=mesh['shot'=4,'mesh'=8] {'mesh'}, use_global_device_ids=true, to_apply=%region_21.0 | all-reduce | flops 1 | bytes 8 | tf_op jit(solution)/shard_map/psum | solution.py:228
  313.9 19.8 %psum.92 = f32[]{:T(128)} all-reduce(f32[]{:T(128)} %fusion.44), channel_id=1, replica_groups=mesh['shot'=4,'mesh'=8] {'mesh'}, use_global_device_ids=true, to_apply=%region_23.0 | all-reduce | flops 1 | bytes 8 | tf_op jit(solution)/shard_map/psum | solution.py:228
  335.7 17.7 %psum.93 = f32[]{:T(128)} all-reduce(f32[]{:T(128)} %get-tuple-element.14), channel_id=1, replica_groups=mesh['shot'=4,'mesh'=8] {'mesh'}, use_global_device_ids=true, to_apply=%region_25.0 | all-reduce | flops 1 | bytes 8 | tf_op jit(solution)/shard_map/psum | solution.py:228
  356.3 19.7 %psum.94 = f32[]{:T(128)} all-reduce(f32[]{:T(128)} %fusion.60), channel_id=1, replica_groups=mesh['shot'=4,'mesh'=8] {'mesh'}, use_global_device_ids=true, to_apply=%region_27.0 | all-reduce | flops 1 | bytes 8 | tf_op jit(solution)/shard_map/psum | solution.py:228
  378.1 17.7 %psum.95 = f32[]{:T(128)} all-reduce(f32[]{:T(128)} %get-tuple-element.12), channel_id=1, replica_groups=mesh['shot'=4,'mesh'=8] {'mesh'}, use_global_device_ids=true, to_apply=%region_29.0 | all-reduce | flops 1 | bytes 8 | tf_op jit(solution)/shard_map/psum | solution.py:228
  (155 shorter events, 63.8 us)
Async XLA Ops:
  7.2 174.6 %all-reduce.3.cloned.1.call-start = ((), (), s32[]{:S(2)}) async-start(), calls=%async_computation | async-start | bytes 286720 | tf_op jit(solution)/shard_map/psum | solution.py:225
  9.8 17.7 %copy-start.2 = (f32[5,6,35,128]{3,2,1,0:T(8,128)S(1)}, f32[5,6,35,128]{3,2,1,0:T(8,128)}, u32[]{:S(2)}) copy-start(f32[5,6,35,128]{3,2,1,0:T(8,128)} %param.37) | copy-start | bytes 1612804
  9.8 17.7 %copy-start.3 = (f32[5,6,35,128]{3,2,1,0:T(8,128)S(1)}, f32[5,6,35,128]{3,2,1,0:T(8,128)}, u32[]{:S(2)}) copy-start(f32[5,6,35,128]{3,2,1,0:T(8,128)} %param.36) | copy-start | bytes 1612804
  13.5 15.6 %copy-start.26 = (s32[4,128]{1,0:T(4,128)S(1)}, s32[4,128]{1,0:T(4,128)}, u32[]{:S(2)}) copy-start(s32[4,128]{1,0:T(4,128)} %param.34) | copy-start | bytes 6148
  17.3 11.8 %copy-start.27 = (s32[4,128]{1,0:T(4,128)S(1)}, s32[4,128]{1,0:T(4,128)}, u32[]{:S(2)}) copy-start(s32[4,128]{1,0:T(4,128)} %param.33) | copy-start | bytes 6148
  17.3 11.8 %copy-start.30 = (s32[15]{0:T(128)S(1)}, s32[15]{0:T(128)}, u32[]{:S(2)}) copy-start(s32[15]{0:T(128)} %constant.67.clone) | copy-start | bytes 184
  17.3 11.8 %copy-start.31 = (s32[15]{0:T(128)S(1)}, s32[15]{0:T(128)}, u32[]{:S(2)}) copy-start(s32[15]{0:T(128)} %constant.66.clone) | copy-start | bytes 184
  17.3 11.8 %copy-start.32 = (s32[15]{0:T(128)S(1)}, s32[15]{0:T(128)}, u32[]{:S(2)}) copy-start(s32[15]{0:T(128)} %constant.65.clone) | copy-start | bytes 184
  17.3 11.8 %copy-start.33 = (s32[15]{0:T(128)S(1)}, s32[15]{0:T(128)}, u32[]{:S(2)}) copy-start(s32[15]{0:T(128)} %constant.64.clone) | copy-start | bytes 184
  17.3 11.8 %copy-start.34 = (s32[15]{0:T(128)S(1)}, s32[15]{0:T(128)}, u32[]{:S(2)}) copy-start(s32[15]{0:T(128)} %constant.63.clone) | copy-start | bytes 184
  17.4 12.0 %copy-start.28 = (f32[4,128]{1,0:T(4,128)S(1)}, f32[4,128]{1,0:T(4,128)}, u32[]{:S(2)}) copy-start(f32[4,128]{1,0:T(4,128)} %param.32) | copy-start | bytes 6148
  17.4 12.0 %copy-start.1 = (f32[1,13,35,128]{3,0,2,1:T(1,128)S(1)}, f32[1,13,35,128]{3,0,2,1:T(1,128)}, u32[]{:S(2)}) copy-start(f32[1,13,35,128]{3,0,2,1:T(1,128)} %param.26) | copy-start | bytes 698884
  17.4 12.0 %copy-start.10 = (f32[3,35,35,1]{2,1,3,0:T(8,128)S(1)}, f32[3,35,35,1]{2,1,3,0:T(8,128)}, u32[]{:S(2)}) copy-start(f32[3,35,35,1]{2,1,3,0:T(8,128)} %constant.74) | copy-start | bytes 44104
  19.8 10.5 %copy-start.25 = (f32[3,3,128]{2,1,0:T(4,128)S(1)}, f32[3,3,128]{2,1,0:T(4,128)}, u32[]{:S(2)}) copy-start(f32[3,3,128]{2,1,0:T(4,128)} %param.30) | copy-start | bytes 13828
  19.8 10.5 %copy-start = (f32[6,35,128]{2,1,0:T(8,128)S(1)}, f32[6,35,128]{2,1,0:T(8,128)}, u32[]{:S(2)}) copy-start(f32[6,35,128]{2,1,0:T(8,128)} %param.28) | copy-start | bytes 322564
  19.8 10.5 %copy-start.16 = (f32[1,2,13,35,128]{4,1,3,2,0:T(2,128)S(1)}, f32[1,2,13,35,128]{4,1,3,2,0:T(2,128)}, u32[]{:S(2)}) copy-start(f32[1,2,13,35,128]{4,1,3,2,0:T(2,128)} %param.27) | copy-start | bytes 1397764
  19.8 19.8 %collective-permute-start.1 = (f32[13,15,64]{1,0,2:T(8,128)}, f32[13,15,64]{1,0,2:T(8,128)}, u32[]{:S(2)}, u32[]{:S(2)}) collective-permute-start(f32[13,15,64]{1,0,2:T(8,128)} %get-tuple-element.23), channel_id=1, source_target_pairs={{1,0},{2,1},{3,2},{4,3},{5,4},{6,5},{7,6},{9,8},{10,9},{11,10},{12... | collective-permute-start | bytes 149768 | tf_op jit(solution)/shard_map/ppermute | solution.py:20
  21.2 27.2 %collective-permute-start = (f32[13,15,64]{1,0,2:T(8,128)}, f32[13,15,64]{1,0,2:T(8,128)}, u32[]{:S(2)}, u32[]{:S(2)}) collective-permute-start(f32[13,15,64]{1,0,2:T(8,128)} %get-tuple-element.22), channel_id=1, source_target_pairs={{0,1},{1,2},{2,3},{3,4},{4,5},{5,6},{6,7},{8,9},{9,10},{10,11},{11... | collective-permute-start | bytes 149768 | tf_op jit(solution)/shard_map/ppermute | solution.py:19
  39.6 33.6 %copy-start.21 = (f32[3,4,128]{2,0,1:T(4,128)}, f32[3,4,128]{2,0,1:T(4,128)S(1)}, u32[]{:S(2)}) copy-start(f32[3,4,128]{2,0,1:T(4,128)S(1)} %copy.154) | copy-start | bytes 18436
  90.9 16.6 %collective-permute-start.3 = (f32[13,15,64]{1,0,2:T(8,128)S(1)}, f32[13,15,64]{1,0,2:T(8,128)}, u32[]{:S(2)}, u32[]{:S(2)}) collective-permute-start(f32[13,15,64]{1,0,2:T(8,128)S(1)} %get-tuple-element.21), channel_id=1, source_target_pairs={{1,0},{2,1},{3,2},{4,3},{5,4},{6,5},{7,6},{9,8},{10,9},{11,10},{12... | collective-permute-start | bytes 149768 | tf_op jit(solution)/shard_map/ppermute | solution.py:20
  92.2 26.7 %collective-permute-start.2 = (f32[13,15,64]{1,0,2:T(8,128)}, f32[13,15,64]{1,0,2:T(8,128)}, u32[]{:S(2)}, u32[]{:S(2)}) collective-permute-start(f32[13,15,64]{1,0,2:T(8,128)} %get-tuple-element.20), channel_id=1, source_target_pairs={{0,1},{1,2},{2,3},{3,4},{4,5},{5,6},{6,7},{8,9},{9,10},{10,11},{11... | collective-permute-start | bytes 149768 | tf_op jit(solution)/shard_map/ppermute | solution.py:19
  146.5 81.4 %copy-start.4 = (f32[1,6,35,128]{3,2,1,0:T(8,128)S(1)}, f32[1,6,35,128]{3,2,1,0:T(8,128)}, u32[]{:S(2)}) copy-start(f32[1,6,35,128]{3,2,1,0:T(8,128)} %get-tuple-element.39) | copy-start | bytes 322564
  146.6 104.0 %copy-start.5 = (f32[1,6,35,128]{3,2,1,0:T(8,128)S(1)}, f32[1,6,35,128]{3,2,1,0:T(8,128)}, u32[]{:S(2)}) copy-start(f32[1,6,35,128]{3,2,1,0:T(8,128)} %get-tuple-element.72) | copy-start | bytes 322564
  146.6 123.8 %copy-start.7 = (f32[1,6,35,128]{3,2,1,0:T(8,128)S(1)}, f32[1,6,35,128]{3,2,1,0:T(8,128)}, u32[]{:S(2)}) copy-start(f32[1,6,35,128]{3,2,1,0:T(8,128)} %get-tuple-element.37) | copy-start | bytes 322564
  (17 other events, 68.5 us)
Sparse Core Ops, SparseCore 0:
  150.0 31.6 all-reduce.2
where the time goes:
time: 406 us; the launch traced here: 405 us
  blocking collectives  190 us (47%)
  local copies, waits for them, and re-layouts  81.3 us (20%)
  waiting for transfers between devices  53.4 us (13%)
  between operations  29.4 us (7%)
  matrix products  19.9 us (5%)
  other arithmetic  16.3 us (4%)
  starting transfers between devices  14.9 us (4%)
    psum x10, blocking collectives, combine_sums(): return lax.psum(values, 'mesh')  190 us
    gather x2, local copies, waits for them, and re-layouts, shards(): turned = ghosts.reshape(fields, face_width * slot_count)[:, flat_index]  34.6 us
    psum x1, waiting for transfers between devices, shards(): total_grad = lax.psum(gradient, 'shot')  31.2 us
    ppermute x2, waiting for transfers between devices, padded(): before = lax.ppermute(last, axis, up)  17.7 us
    ppermute x2, starting transfers between devices, padded(): before = lax.ppermute(last, axis, up)  12.1 us
    reshape x4, local copies, waits for them, and re-layouts, shards(): flat_trace = inner_trace.reshape(fields, face_width, 4 * elements)  8.56 us
  transfers between devices with their start and end apart: 5, of which 4 were waited for; matrix products, arithmetic and copies ran while one was open for 5% of the time, Pallas kernels for 0%

commit v1 on v0

--- a/solution.py
+++ b/solution.py
@@ -222,7 +222,7 @@
         gradient = gradient + STEP_SIZE * kernel_term(
             adjoint, forward_states[0, step_index], coupling, metric, derivs
         )
-    total_grad = lax.psum(gradient, "shot")
+    total_grad = lax.all_gather(gradient, "shot").sum(axis=0)
 
     def combine_sums(values):
         return lax.psum(values, "mesh")

time: 406 us -> 363 us (0.89)
  waiting for transfers between devices: 53.4 us -> 21.5 us
  between operations: 29.4 us -> 15.9 us
  blocking collectives: 190 us -> 196 us
    psum x1 -> x0, waiting for transfers between devices: 31.2 us -> none  [shards(): total_grad = lax.psum(gradient, 'shot')]
    all_gather x0 -> x1, blocking collectives: none -> 7.02 us  [shards(): total_grad = lax.all_gather(gradient, 'shot').sum(axis=0)]
  transfers between devices with their start and end apart: 5 -> 4, of which waited for: 4 -> 3; matrix products, arithmetic and copies ran while one was open for 5% -> 5% of each run, Pallas kernels for 0% -> 0%
where the time goes in v1:
time: 363 us; the launch traced here: 362 us
  blocking collectives  196 us (54%)
  local copies, waits for them, and re-layouts  79.6 us (22%)
  waiting for transfers between devices  21.5 us (6%)
  matrix products  18.4 us (5%)
  between operations  15.9 us (4%)
  other arithmetic  15.7 us (4%)
  starting transfers between devices  14.8 us (4%)
    psum x10, blocking collectives, combine_sums(): return lax.psum(values, 'mesh')  189 us
    gather x2, local copies, waits for them, and re-layouts, shards(): turned = ghosts.reshape(fields, face_width * slot_count)[:, flat_index]  34.6 us
    ppermute x2, waiting for transfers between devices, padded(): before = lax.ppermute(last, axis, up)  17 us
    ppermute x2, starting transfers between devices, padded(): before = lax.ppermute(last, axis, up)  12.2 us
    reshape x4, local copies, waits for them, and re-layouts, shards(): flat_trace = inner_trace.reshape(fields, face_width, 4 * elements)  8.56 us
  transfers between devices with their start and end apart: 4, of which 3 were waited for; matrix products, arithmetic and copies ran while one was open for 5% of the time, Pallas kernels for 0%

profile of v1, /device:TPU:0, one launch (start us, length us, event | category | flops | bytes accessed | tf_op | source)
XLA Modules:
  0.0 361.6 jit_solution(3339148320260790142)
XLA Ops:
  3.3 3.6 %copy.157 = f32[13,15,512]{1,0,2:T(8,128)} copy(f32[13,15,512]{2,1,0:T(8,128)S(1)} %reshape.294) | data formatting | bytes 798720 | tf_op jit(solution)/shard_map/reshape | solution.py:210
  12.9 6.3 %collective-permute-start = (f32[13,15,64]{1,0,2:T(8,128)}, f32[13,15,64]{1,0,2:T(8,128)}, u32[]{:S(2)}, u32[]{:S(2)}) collective-permute-start(f32[13,15,64]{1,0,2:T(8,128)} %get-tuple-element.24), channel_id=1, source_target_pairs={{0,1},{1,2},{2,3},{3,4},{4,5},{5,6},{6,7},{8,9},{9,10},{10,11},{11... | collective-permute-start | bytes 149768 | tf_op jit(solution)/shard_map/ppermute | solution.py:19
  33.2 6.9 %collective-permute-done = f32[13,15,64]{1,0,2:T(8,128)} collective-permute-done((f32[13,15,64]{1,0,2:T(8,128)}, f32[13,15,64]{1,0,2:T(8,128)}, u32[]{:S(2)}, u32[]{:S(2)}) %collective-permute-start) | collective-permute-done | bytes 49952 | tf_op jit(solution)/shard_map/ppermute | solution.py:19
  42.9 3.2 copy.160
  46.1 17.3 %gather_fusion.3 = f32[7680,13]{1,0:T(8,128)} fusion(f32[13,9600]{0,1:T(8,128)} %bitcast.313, s32[8192]{0:T(1024)S(1)} %pad_clamp_fusion), kind=kCustom, calls=%fused_computation.3 | custom fusion | bytes 829440 | tf_op jit(solution)/shard_map/gather | solution.py:216
  66.3 3.6 %fusion.1 = f32[13,15,4,128]{3,0,2,1:T(8,128)S(1)} fusion(f32[6,15,4,128]{3,0,2,1:T(8,128)} %bitcast.325, f32[13,15,4,128]{3,0,2,1:T(8,128)S(1)} %sub.44, f32[3,4,128]{2,0,1:T(4,128)S(1)} %copy.154, f32[3,6,13,13]{3,2,1,0:T(8,128)S(1)} %copy-done.10), kind=kOutput, calls=%fused_computation.10 | convolution fusion | flops 281748480 | bytes 1001352 | tf_op jit(solution)/shard_map/dpfg,dfnxe->pgnxe/dot_general | solution.py:143
  74.4 3.6 %copy.170 = f32[13,15,512]{1,0,2:T(8,128)} copy(f32[13,15,512]{2,1,0:T(8,128)S(1)} %reshape.297) | data formatting | bytes 798720 | tf_op jit(solution)/shard_map/reshape | solution.py:210
  78.0 3.9 %gather_fusion.5 = f32[128,13,15]{2,1,0:T(8,128)} fusion(f32[13,15,512]{1,0,2:T(8,128)} %copy.170, s32[1024]{0:T(1024)} %pad_clamp_fusion.1), kind=kCustom, calls=%fused_computation.5 | custom fusion | bytes 200192 | tf_op jit(solution)/shard_map/gather | solution.py:211
  85.5 5.8 %collective-permute-start.2 = (f32[13,15,64]{1,0,2:T(8,128)}, f32[13,15,64]{1,0,2:T(8,128)}, u32[]{:S(2)}, u32[]{:S(2)}) collective-permute-start(f32[13,15,64]{1,0,2:T(8,128)} %get-tuple-element.22), channel_id=1, source_target_pairs={{0,1},{1,2},{2,3},{3,4},{4,5},{5,6},{6,7},{8,9},{9,10},{10,11},{11... | collective-permute-start | bytes 149768 | tf_op jit(solution)/shard_map/ppermute | solution.py:19
  96.3 4.5 %collective-permute-done.3 = f32[13,15,64]{1,0,2:T(8,128)} collective-permute-done((f32[13,15,64]{1,0,2:T(8,128)S(1)}, f32[13,15,64]{1,0,2:T(8,128)}, u32[]{:S(2)}, u32[]{:S(2)}) %collective-permute-start.3) | collective-permute-done | bytes 49952 | tf_op jit(solution)/shard_map/ppermute | solution.py:20
  102.1 10.1 %collective-permute-done.2 = f32[13,15,64]{1,0,2:T(8,128)} collective-permute-done((f32[13,15,64]{1,0,2:T(8,128)}, f32[13,15,64]{1,0,2:T(8,128)}, u32[]{:S(2)}, u32[]{:S(2)}) %collective-permute-start.2) | collective-permute-done | bytes 49952 | tf_op jit(solution)/shard_map/ppermute | solution.py:19
  113.5 3.2 copy.173
  116.8 17.3 %gather_fusion.6 = f32[7680,13]{1,0:T(8,128)} fusion(f32[13,9600]{0,1:T(8,128)} %bitcast.312, s32[8192]{0:T(1024)S(1)} %pad_clamp_fusion), kind=kCustom, calls=%fused_computation.6 | custom fusion | bytes 829440 | tf_op jit(solution)/shard_map/gather | solution.py:216
  142.5 7.0 %all-gather = f32[24,35,128]{2,1,0:T(8,128)S(1)} all-gather(f32[6,35,128]{2,1,0:T(8,128)S(1)} %copy.186), channel_id=2, replica_groups=mesh['shot'=4,'mesh'=8] {'shot'}, dimensions={0}, use_global_device_ids=true | all-gather | bytes 537600 | tf_op jit(solution)/shard_map/all_gather | solution.py:225
  150.2 20.9 %all-reduce = (f32[]{:T(128)}, f32[6]{0:T(128)S(1)}) all-reduce(f32[]{:T(128)} %multiply_reduce_fusion.1, f32[6]{0:T(128)S(1)} %copy-done.33), channel_id=1, replica_groups=mesh['shot'=4,'mesh'=8] {'mesh'}, use_global_device_ids=true, to_apply=%region_11.0 | all-reduce | flops 7 | bytes 56 | tf_op jit(solution)/shard_map/psum | solution.py:228
  173.7 17.7 %psum.79 = f32[]{:T(128)} all-reduce(f32[]{:T(128)} %fusion.51), channel_id=1, replica_groups=mesh['shot'=4,'mesh'=8] {'mesh'}, use_global_device_ids=true, to_apply=%region_13.0 | all-reduce | flops 1 | bytes 8 | tf_op jit(solution)/shard_map/psum | solution.py:228
  193.4 19.7 %psum.80 = f32[]{:T(128)} all-reduce(f32[]{:T(128)} %get-tuple-element.20), channel_id=1, replica_groups=mesh['shot'=4,'mesh'=8] {'mesh'}, use_global_device_ids=true, to_apply=%region_15.0 | all-reduce | flops 1 | bytes 8 | tf_op jit(solution)/shard_map/psum | solution.py:228
  215.1 17.7 %psum.81 = f32[]{:T(128)} all-reduce(f32[]{:T(128)} %fusion.43), channel_id=1, replica_groups=mesh['shot'=4,'mesh'=8] {'mesh'}, use_global_device_ids=true, to_apply=%region_17.0 | all-reduce | flops 1 | bytes 8 | tf_op jit(solution)/shard_map/psum | solution.py:228
  234.8 19.7 %psum.82 = f32[]{:T(128)} all-reduce(f32[]{:T(128)} %get-tuple-element.18), channel_id=1, replica_groups=mesh['shot'=4,'mesh'=8] {'mesh'}, use_global_device_ids=true, to_apply=%region_19.0 | all-reduce | flops 1 | bytes 8 | tf_op jit(solution)/shard_map/psum | solution.py:228
  257.8 17.7 %psum.83 = f32[]{:T(128)} all-reduce(f32[]{:T(128)} %get-tuple-element.16), channel_id=1, replica_groups=mesh['shot'=4,'mesh'=8] {'mesh'}, use_global_device_ids=true, to_apply=%region_21.0 | all-reduce | flops 1 | bytes 8 | tf_op jit(solution)/shard_map/psum | solution.py:228
  277.6 19.7 %psum.84 = f32[]{:T(128)} all-reduce(f32[]{:T(128)} %fusion.42), channel_id=1, replica_groups=mesh['shot'=4,'mesh'=8] {'mesh'}, use_global_device_ids=true, to_apply=%region_23.0 | all-reduce | flops 1 | bytes 8 | tf_op jit(solution)/shard_map/psum | solution.py:228
  299.3 17.7 %psum.85 = f32[]{:T(128)} all-reduce(f32[]{:T(128)} %get-tuple-element.14), channel_id=1, replica_groups=mesh['shot'=4,'mesh'=8] {'mesh'}, use_global_device_ids=true, to_apply=%region_25.0 | all-reduce | flops 1 | bytes 8 | tf_op jit(solution)/shard_map/psum | solution.py:228
  319.9 19.7 %psum.86 = f32[]{:T(128)} all-reduce(f32[]{:T(128)} %fusion.50), channel_id=1, replica_groups=mesh['shot'=4,'mesh'=8] {'mesh'}, use_global_device_ids=true, to_apply=%region_27.0 | all-reduce | flops 1 | bytes 8 | tf_op jit(solution)/shard_map/psum | solution.py:228
  341.6 17.7 %psum.87 = f32[]{:T(128)} all-reduce(f32[]{:T(128)} %get-tuple-element.12), channel_id=1, replica_groups=mesh['shot'=4,'mesh'=8] {'mesh'}, use_global_device_ids=true, to_apply=%region_29.0 | all-reduce | flops 1 | bytes 8 | tf_op jit(solution)/shard_map/psum | solution.py:228
  (150 shorter events, 60.6 us)
Async XLA Ops:
  2.9 4.0 %copy-start.32 = (s32[128]{0:T(128)S(1)}, s32[128]{0:T(128)}, u32[]{:S(2)}) copy-start(s32[128]{0:T(128)} %param.35) | copy-start | bytes 1540
  3.2 15.9 %copy-start.1 = (f32[5,6,35,128]{3,2,1,0:T(8,128)S(1)}, f32[5,6,35,128]{3,2,1,0:T(8,128)}, u32[]{:S(2)}) copy-start(f32[5,6,35,128]{3,2,1,0:T(8,128)} %param.37) | copy-start | bytes 1612804
  3.3 16.6 %copy-start.2 = (f32[5,6,35,128]{3,2,1,0:T(8,128)S(1)}, f32[5,6,35,128]{3,2,1,0:T(8,128)}, u32[]{:S(2)}) copy-start(f32[5,6,35,128]{3,2,1,0:T(8,128)} %param.36) | copy-start | bytes 1612804
  6.9 14.8 %copy-start.3 = (f32[1,13,35,128]{3,0,2,1:T(1,128)S(1)}, f32[1,13,35,128]{3,0,2,1:T(1,128)}, u32[]{:S(2)}) copy-start(f32[1,13,35,128]{3,0,2,1:T(1,128)} %param.26) | copy-start | bytes 698884
  6.9 15.6 %copy-start = (f32[6,35,128]{2,1,0:T(8,128)S(1)}, f32[6,35,128]{2,1,0:T(8,128)}, u32[]{:S(2)}) copy-start(f32[6,35,128]{2,1,0:T(8,128)} %param.28) | copy-start | bytes 322564
  10.4 10.2 %copy-start.29 = (s32[4,128]{1,0:T(4,128)S(1)}, s32[4,128]{1,0:T(4,128)}, u32[]{:S(2)}) copy-start(s32[4,128]{1,0:T(4,128)} %param.34) | copy-start | bytes 6148
  10.5 10.2 %copy-start.30 = (s32[4,128]{1,0:T(4,128)S(1)}, s32[4,128]{1,0:T(4,128)}, u32[]{:S(2)}) copy-start(s32[4,128]{1,0:T(4,128)} %param.33) | copy-start | bytes 6148
  10.5 11.2 %copy-start.31 = (f32[4,128]{1,0:T(4,128)S(1)}, f32[4,128]{1,0:T(4,128)}, u32[]{:S(2)}) copy-start(f32[4,128]{1,0:T(4,128)} %param.32) | copy-start | bytes 6148
  10.5 11.2 %copy-start.6 = (f32[3,35,35,1]{2,1,3,0:T(8,128)S(1)}, f32[3,35,35,1]{2,1,3,0:T(8,128)}, u32[]{:S(2)}) copy-start(f32[3,35,35,1]{2,1,3,0:T(8,128)} %constant.74) | copy-start | bytes 44104
  10.5 12.0 %copy-start.28 = (f32[3,3,128]{2,1,0:T(4,128)S(1)}, f32[3,3,128]{2,1,0:T(4,128)}, u32[]{:S(2)}) copy-start(f32[3,3,128]{2,1,0:T(4,128)} %param.30) | copy-start | bytes 13828
  10.5 12.1 %copy-start.14 = (f32[1,2,13,35,128]{4,1,3,2,0:T(2,128)S(1)}, f32[1,2,13,35,128]{4,1,3,2,0:T(2,128)}, u32[]{:S(2)}) copy-start(f32[1,2,13,35,128]{4,1,3,2,0:T(2,128)} %param.27) | copy-start | bytes 1397764
  11.6 20.3 %collective-permute-start.1 = (f32[13,15,64]{1,0,2:T(8,128)}, f32[13,15,64]{1,0,2:T(8,128)}, u32[]{:S(2)}, u32[]{:S(2)}) collective-permute-start(f32[13,15,64]{1,0,2:T(8,128)} %get-tuple-element.25), channel_id=1, source_target_pairs={{1,0},{2,1},{3,2},{4,3},{5,4},{6,5},{7,6},{9,8},{10,9},{11,10},{12... | collective-permute-start | bytes 149768 | tf_op jit(solution)/shard_map/ppermute | solution.py:20
  12.9 27.2 %collective-permute-start = (f32[13,15,64]{1,0,2:T(8,128)}, f32[13,15,64]{1,0,2:T(8,128)}, u32[]{:S(2)}, u32[]{:S(2)}) collective-permute-start(f32[13,15,64]{1,0,2:T(8,128)} %get-tuple-element.24), channel_id=1, source_target_pairs={{0,1},{1,2},{2,3},{3,4},{4,5},{5,6},{6,7},{8,9},{9,10},{10,11},{11... | collective-permute-start | bytes 149768 | tf_op jit(solution)/shard_map/ppermute | solution.py:19
  26.9 5.0 %copy-start.27 = (f32[3,4,128]{2,1,0:T(4,128)S(1)}, f32[3,4,128]{2,1,0:T(4,128)}, u32[]{:S(2)}) copy-start(f32[3,4,128]{2,1,0:T(4,128)} %param.31) | copy-start | bytes 18436
  31.9 34.4 %copy-start.25 = (f32[3,4,128]{2,0,1:T(4,128)}, f32[3,4,128]{2,0,1:T(4,128)S(1)}, u32[]{:S(2)}) copy-start(f32[3,4,128]{2,0,1:T(4,128)S(1)} %copy.154) | copy-start | bytes 18436
  66.3 4.6 %copy-start.7 = (f32[3,35,35,1]{2,1,3,0:T(8,128)S(1)}, f32[3,35,35,1]{2,1,3,0:T(8,128)}, u32[]{:S(2)}) copy-start(f32[3,35,35,1]{2,1,3,0:T(8,128)} %constant.74) | copy-start | bytes 44104
  74.4 17.0 %copy-start.20 = (f32[128]{0:T(128)S(1)}, f32[128]{0:T(128)}, u32[]{:S(2)}) copy-start(f32[128]{0:T(128)} %copy-done.19) | copy-start | bytes 1540
  81.9 10.2 %copy-start.9 = (f32[3,13,35,128,1]{3,2,1,0,4:T(8,128)S(1)}, f32[3,13,35,128,1]{3,2,1,0,4:T(8,128)}, u32[]{:S(2)}) copy-start(f32[3,13,35,128,1]{3,2,1,0,4:T(8,128)} %maximum_bitcast_fusion.2) | copy-start | bytes 2096644
  81.9 10.3 %copy-start.11 = (f32[3,6,13,13]{3,2,1,0:T(8,128)S(1)}, f32[3,6,13,13]{3,2,1,0:T(8,128)}, u32[]{:S(2)}) copy-start(f32[3,6,13,13]{3,2,1,0:T(8,128)} %param.29) | copy-start | bytes 36508
  84.1 10.6 %copy-start.5 = (f32[6,35,128]{2,0,1:T(8,128)S(1)}, f32[6,35,128]{2,0,1:T(8,128)}, u32[]{:S(2)}) copy-start(f32[6,35,128]{2,0,1:T(8,128)} %copy-done.4) | copy-start | bytes 322564
  84.1 16.7 %collective-permute-start.3 = (f32[13,15,64]{1,0,2:T(8,128)S(1)}, f32[13,15,64]{1,0,2:T(8,128)}, u32[]{:S(2)}, u32[]{:S(2)}) collective-permute-start(f32[13,15,64]{1,0,2:T(8,128)S(1)} %get-tuple-element.23), channel_id=1, source_target_pairs={{1,0},{2,1},{3,2},{4,3},{5,4},{6,5},{7,6},{9,8},{10,9},{11,10},{12... | collective-permute-start | bytes 149768 | tf_op jit(solution)/shard_map/ppermute | solution.py:20
  85.5 26.7 %collective-permute-start.2 = (f32[13,15,64]{1,0,2:T(8,128)}, f32[13,15,64]{1,0,2:T(8,128)}, u32[]{:S(2)}, u32[]{:S(2)}) collective-permute-start(f32[13,15,64]{1,0,2:T(8,128)} %get-tuple-element.22), channel_id=1, source_target_pairs={{0,1},{1,2},{2,3},{3,4},{4,5},{5,6},{6,7},{8,9},{9,10},{10,11},{11... | collective-permute-start | bytes 149768 | tf_op jit(solution)/shard_map/ppermute | solution.py:19
  139.8 10.4 %copy-start.33 = (f32[6]{0:T(128)S(1)}, f32[6]{0:T(128)}, u32[]{:S(2)}) copy-start(f32[6]{0:T(128)} %pad_maximum_fusion.2) | copy-start | bytes 76
  149.5 211.2 %copy-start.13 = (f32[6,35,128]{2,1,0:T(8,128)S(1)}, f32[6,35,128]{2,1,0:T(8,128)}, u32[]{:S(2)}) copy-start(f32[6,35,128]{2,1,0:T(8,128)} %slice_bitcast_fusion) | copy-start | bytes 322564
  (14 other events, 37.8 us)
